TPU v7x, 32 devices: a whole 2x2x4 slice. The times are simulated.
32 devices in a mesh: region: 2 (over y), tile: 4 (over z), corner: 2 (over x), kern: 2 (over core).
Axes of the slice: x: 2, y: 2, z: 4, core: 2. Of those that a mesh axis runs over, the one named last changes fastest.
Arguments:
- tile_mask: bfloat16 [16, 256, 256], P(('region', 'tile')), parts along dimension 0, may hold values from -1 to 1
- master_mask: bfloat16 [8, 256, 256], P(('region', 'tile')), parts along dimension 0, may hold values from -1 to 1
- target: bfloat16 [16, 256, 256], P(('region', 'tile')), parts along dimension 0, may hold values from 0 to 1
- inst_master: int32 [16], P(('region', 'tile')), parts along dimension 0, may hold values from 0 to 3, as said below
- inst_shift: int32 [16, 2], P(('region', 'tile')), parts along dimension 0, may hold values from 0 to 255
- kernels: float32 [2, 12, 2, 32, 32], P('corner'), may hold values from -24 to 24
- kernel_weight: float32 [2, 12], P('corner'), may hold values from 0.05 to 1
- corner_dose: float32 [2], P('corner'), may hold values from 0.6 to 1.6
Outputs:
- tile_grad: float32 [16, 256, 256], P(('region', 'tile')), parts along dimension 0
- master_grad: float32 [8, 256, 256], P(('region', 'tile')), parts along dimension 0
There are 2 independent parts, one for each index of `region`. A program takes and returns all parts, laid end to end along the dimension named above; an argument that names none is the same for every part. Nothing has to cross between parts.
Inputs may be any that keep to these rules, and one draw needn't show every extreme that they name: `inst_master`: each master cell is placed in exactly 2 tiles.
All inputs are finite; a program needn't handle non-finite values.
Results may differ from a plain program's by a relative error of at most 0.0003.
Values may be sent and summed in bfloat16 or wider, within the bound.
No kernel may reach another device: no remote copies, remote signals or barrier semaphores. Data moves between devices by JAX's collectives and lax.ppermute only.
A program may use at most 64 MiB of HBM per device.

v0:
```python
import math
import numpy as np
import jax
import jax.numpy as jnp
from jax import lax
from jax.sharding import PartitionSpec as P

P_SIZE = 256
B = 32
precise = lax.Precision.HIGHEST
steepness = 3.0
threshold = 1.0


def band_tables():
    freq = np.arange(B, dtype=np.int64) - B // 2
    pixel = np.arange(P_SIZE, dtype=np.int64)
    angle = (
        2.0 * math.pi / P_SIZE * np.mod(freq[:, None] * pixel[None, :], P_SIZE).astype(np.float64)
    )
    return (jnp.asarray(np.cos(angle), jnp.float32), jnp.asarray(-np.sin(angle), jnp.float32))


def phase_ramp(shift):
    freq = jnp.arange(B, dtype=jnp.int32) - B // 2
    total = (
        freq[None, :, None] * shift[:, 0][:, None, None]
        + freq[None, None, :] * shift[:, 1][:, None, None]
    )
    angle = 2.0 * math.pi / P_SIZE * jnp.mod(total, P_SIZE).astype(jnp.float32)
    return (jnp.cos(angle), -jnp.sin(angle))


def spectra(masks, cos_tab, sin_tab):
    rows_re = jnp.einsum("bx,nxy->nby", cos_tab, masks, precision=precise)
    rows_im = jnp.einsum("bx,nxy->nby", sin_tab, masks, precision=precise)
    spec_re = jnp.einsum("nby,cy->nbc", rows_re, cos_tab, precision=precise) - jnp.einsum(
        "nby,cy->nbc", rows_im, sin_tab, precision=precise
    )
    spec_im = jnp.einsum("nby,cy->nbc", rows_re, sin_tab, precision=precise) + jnp.einsum(
        "nby,cy->nbc", rows_im, cos_tab, precision=precise
    )
    return (spec_re, spec_im)


def back_pixels(x_re, x_im, cos_tab, sin_tab):
    half_re = jnp.einsum("bx,nbc->nxc", cos_tab, x_re, precision=precise) + jnp.einsum(
        "bx,nbc->nxc", sin_tab, x_im, precision=precise
    )
    half_im = jnp.einsum("bx,nbc->nxc", cos_tab, x_im, precision=precise) - jnp.einsum(
        "bx,nbc->nxc", sin_tab, x_re, precision=precise
    )
    return jnp.einsum("nxc,cy->nxy", half_re, cos_tab, precision=precise) + jnp.einsum(
        "nxc,cy->nxy", half_im, sin_tab, precision=precise
    )


def on_device(
    tile_mask, master_mask, target, inst_master, inst_shift, kernels, kernel_weight, corner_dose
):
    cos_tab, sin_tab = band_tables()
    scale = 1.0 / (P_SIZE * P_SIZE)
    local_tiles = tile_mask.shape[0]
    local_masters = master_mask.shape[0]
    tile_count = lax.axis_size("tile")
    tile_pos = lax.axis_index("tile")
    kern_count = lax.axis_size("kern")
    kern_pos = lax.axis_index("kern")
    per_dev = local_tiles // kern_count
    first = kern_pos * per_dev
    region_tiles = tile_count * local_tiles
    region_masters = tile_count * local_masters
    with jax.named_scope("master_spectra"):
        own_re, own_im = spectra(master_mask.astype(jnp.float32), cos_tab, sin_tab)
        own = jnp.stack([own_re, own_im], axis=1)
        every = lax.all_gather(own, "tile", axis=0, tiled=True)
    with jax.named_scope("tile_spectra"):
        mine_mask = lax.dynamic_slice_in_dim(tile_mask, first, per_dev, 0)
        goal = lax.dynamic_slice_in_dim(target, first, per_dev, 0).astype(jnp.float32)
        mine_master = lax.dynamic_slice_in_dim(inst_master, first, per_dev, 0)
        mine_shift = lax.dynamic_slice_in_dim(inst_shift, first, per_dev, 0)
        tile_re, tile_im = spectra(mine_mask.astype(jnp.float32), cos_tab, sin_tab)
        ph_re, ph_im = phase_ramp(mine_shift)
        pick = (
            mine_master[:, None] == jnp.arange(region_masters, dtype=jnp.int32)[None, :]
        ).astype(jnp.float32)
        sel = jnp.sum(pick[:, :, None, None, None] * every[None], axis=1)
        sel_re = sel[:, 0]
        sel_im = sel[:, 1]
        spec_re = tile_re + (ph_re * sel_re - ph_im * sel_im)
        spec_im = tile_im + (ph_re * sel_im + ph_im * sel_re)
    dose = corner_dose[0]
    h_re = kernels[0, :, 0]
    h_im = kernels[0, :, 1]
    weights = kernel_weight[0]
    with jax.named_scope("forward_fields"):
        x_re = h_re[:, None] * spec_re[None] - h_im[:, None] * spec_im[None]
        x_im = h_re[:, None] * spec_im[None] + h_im[:, None] * spec_re[None]
        half_re = jnp.einsum("bx,knbc->knxc", cos_tab, x_re, precision=precise) + jnp.einsum(
            "bx,knbc->knxc", sin_tab, x_im, precision=precise
        )
        half_im = jnp.einsum("bx,knbc->knxc", cos_tab, x_im, precision=precise) - jnp.einsum(
            "bx,knbc->knxc", sin_tab, x_re, precision=precise
        )
        f_re = (
            jnp.einsum("knxc,cy->knxy", half_re, cos_tab, precision=precise)
            + jnp.einsum("knxc,cy->knxy", half_im, sin_tab, precision=precise)
        ) * scale
        f_im = (
            jnp.einsum("knxc,cy->knxy", half_im, cos_tab, precision=precise)
            - jnp.einsum("knxc,cy->knxy", half_re, sin_tab, precision=precise)
        ) * scale
    with jax.named_scope("resist_sensitivity"):
        intensity = jnp.sum(weights[:, None, None, None] * (f_re * f_re + f_im * f_im), axis=0)
        resist = jax.nn.sigmoid(steepness * (dose * intensity - threshold))
        sens = 2.0 * (resist - goal) * resist * (1.0 - resist) * steepness * dose
    with jax.named_scope("adjoint_spectra"):
        g_re = (2.0 * weights)[:, None, None, None] * sens[None] * f_re
        g_im = (2.0 * weights)[:, None, None, None] * sens[None] * f_im
        mid_re = jnp.einsum("knxy,cy->knxc", g_re, cos_tab, precision=precise) - jnp.einsum(
            "knxy,cy->knxc", g_im, sin_tab, precision=precise
        )
        mid_im = jnp.einsum("knxy,cy->knxc", g_re, sin_tab, precision=precise) + jnp.einsum(
            "knxy,cy->knxc", g_im, cos_tab, precision=precise
        )
        out_re = (
            jnp.einsum("bx,knxc->knbc", cos_tab, mid_re, precision=precise)
            - jnp.einsum("bx,knxc->knbc", sin_tab, mid_im, precision=precise)
        ) * scale
        out_im = (
            jnp.einsum("bx,knxc->knbc", cos_tab, mid_im, precision=precise)
            + jnp.einsum("bx,knxc->knbc", sin_tab, mid_re, precision=precise)
        ) * scale
        grad_re = jnp.sum(h_re[:, None] * out_re + h_im[:, None] * out_im, axis=0)
        grad_im = jnp.sum(h_re[:, None] * out_im - h_im[:, None] * out_re, axis=0)
    with jax.named_scope("gradient_exchange"):
        back_re = ph_re * grad_re + ph_im * grad_im
        back_im = ph_re * grad_im - ph_im * grad_re
        tile_slot = tile_pos * local_tiles + first + jnp.arange(per_dev, dtype=jnp.int32)
        tile_pick = (
            tile_slot[:, None] == jnp.arange(region_tiles, dtype=jnp.int32)[None, :]
        ).astype(jnp.float32)
        own_grad = jnp.stack([grad_re, grad_im], axis=1)
        own_back = jnp.stack([back_re, back_im], axis=1)
        tile_part = jnp.sum(tile_pick[:, :, None, None, None] * own_grad[:, None], axis=0)
        master_part = jnp.sum(pick[:, :, None, None, None] * own_back[:, None], axis=0)
        slots = jnp.concatenate([tile_part, master_part], axis=0)
        summed = lax.psum(slots, ("tile", "corner", "kern"))
        mine_tiles = lax.dynamic_slice_in_dim(summed, tile_pos * local_tiles, local_tiles, 0)
        mine_masters = lax.dynamic_slice_in_dim(
            summed, region_tiles + tile_pos * local_masters, local_masters, 0
        )
    with jax.named_scope("pixel_gradients"):
        tile_grad = back_pixels(mine_tiles[:, 0], mine_tiles[:, 1], cos_tab, sin_tab)
        master_grad = back_pixels(mine_masters[:, 0], mine_masters[:, 1], cos_tab, sin_tab)
    return (tile_grad, master_grad)


def solution(mesh):
    return jax.shard_map(
        on_device,
        mesh=mesh,
        in_specs=(
            P(("region", "tile"), None, None),
            P(("region", "tile"), None, None),
            P(("region", "tile"), None, None),
            P(("region", "tile")),
            P(("region", "tile"), None),
            P("corner", None, None, None, None),
            P("corner", None),
            P("corner"),
        ),
        out_specs=(P(("region", "tile"), None, None), P(("region", "tile"), None, None)),
        check_vma=False,
    )
```

profile of v0, /device:TPU:0, one launch (start us, length us, event | category | flops | bytes accessed | tf_op | source)
XLA Modules:
  0.0 185.2 jit_solution(1260496238623281663)
XLA Ops:
  7.3 1.1 fusion.41
  8.4 1.1 fusion.39
  9.5 0.9 fusion.81
  11.4 1.0 convolution_bitcast_fusion.1
  12.4 1.0 convolution_bitcast_fusion
  16.5 1.3 dynamic_slice.20
  18.5 0.9 fusion.26
  19.4 0.9 fusion.27
  20.4 15.1 %all_gather.3 = f32[4,2,32,32]{3,2,1,0:T(8,128)S(1)} all-gather(f32[1,2,32,32]{3,2,1,0:T(8,128)S(1)} %pad_maximum_fusion.1), channel_id=1, replica_groups=mesh['region'=2,'tile'=4,'corner'=2,'kern'=2] {'tile'}, dimensions={0}, use_global_device_ids=true | all-gather | bytes 40960 | tf_op jit(solution)/shard_map/master_spectra/all_gather | solution.py:76
  35.4 1.3 fusion.75
  36.8 0.9 fusion.28
  37.8 0.9 fusion.25
  38.8 1.1 fusion.77
  42.0 2.7 %fusion.83 = f32[12,256,256]{2,1,0:T(8,128)S(1)} fusion(f32[12,256,32]{1,2,0:T(8,128)S(1)} %fusion.15, f32[32,256,1]{1,0,2:T(8,128)S(1)} %copy-done.6), kind=kOutput, calls=%fused_computation.143 | convolution fusion | flops 301989888 | bytes 3571712 | tf_op jit(solution)/shard_map/forward_fields/knxc,cy->knxy/dot_general | solution.py:106
  44.8 4.3 %fusion.84 = f32[12,256,256]{2,1,0:T(8,128)} fusion(f32[12,256,32]{1,2,0:T(8,128)S(1)} %fusion.14, f32[32,256,1]{1,0,2:T(8,128)S(1)} %copy-done.6), kind=kOutput, calls=%fused_computation.144 | convolution fusion | flops 301989888 | bytes 3571712 | tf_op jit(solution)/shard_map/forward_fields/knxc,cy->knxy/dot_general | solution.py:110
  49.1 2.7 %add_multiply_fusion = f32[12,256,256]{2,1,0:T(8,128)S(1)} fusion(f32[12,256,256]{2,1,0:T(8,128)S(1)} %fusion.83, f32[12,256,32]{1,2,0:T(8,128)S(1)} %fusion.14, f32[32,256,1]{1,0,2:T(8,128)S(1)} %copy-done.5), kind=kOutput, calls=%fused_computation.4 | convolution fusion | flops 303562752 | bytes 6717440 | tf_op jit(solution)/shard_map/forward_fields/knxc,cy->knxy/dot_general | solution.py:107
  52.5 5.6 %multiply_reduce_fusion = (f32[256,256]{1,0:T(8,128)S(1)}, f32[12,256,256]{2,1,0:T(8,128)S(1)}) fusion(f32[12,256,256]{2,1,0:T(8,128)S(1)} %add_multiply_fusion, f32[12]{0:T(128)S(1)} %bitcast.235, f32[12,256,256]{2,1,0:T(8,128)} %fusion.84, f32[12,256,32]{1,2,0:T(8,128)} %copy-done.7, f32[32,256,1]{1,0,2:T(8,128)S(1)} %copy-done.5), kind=kOutput, calls=%fused_computation.2 | convolution fusion | flops 307429376 | bytes 10125360 | tf_op jit(solution)/shard_map/forward_fields/knxc,cy->knxy/dot_general | solution.py:111
  58.3 3.3 %fusion = f32[12,256,32]{1,2,0:T(8,128)S(1)} fusion(f32[32,256,1]{1,0,2:T(8,128)S(1)} %copy-done.5, f32[12,256,256]{2,1,0:T(8,128)S(1)} %add_multiply_fusion, f32[256,256]{1,0:T(8,128)S(1)} %fusion.32, f32[12]{0:T(128)S(1)} %broadcast_multiply_fusion.2), kind=kOutput, calls=%fused_computation.5 | convolution fusion | flops 303562752 | bytes 3833904 | tf_op jit(solution)/shard_map/adjoint_spectra/knxy,cy->knxc/dot_general | solution.py:123
  61.6 3.3 %fusion.1 = f32[12,256,32]{1,2,0:T(8,128)S(1)} fusion(f32[32,256,1]{1,0,2:T(8,128)S(1)} %copy-done.6, f32[12,256,256]{2,1,0:T(8,128)S(1)} %add_multiply_fusion, f32[256,256]{1,0:T(8,128)S(1)} %fusion.32, f32[12]{0:T(128)S(1)} %broadcast_multiply_fusion.2), kind=kOutput, calls=%fused_computation.6 | convolution fusion | flops 303562752 | bytes 3833904 | tf_op jit(solution)/shard_map/adjoint_spectra/knxy,cy->knxc/dot_general | solution.py:120
  64.8 3.3 %fusion.13 = f32[12,256,32]{1,2,0:T(8,128)S(1)} fusion(f32[12,256,32]{1,2,0:T(8,128)S(1)} %fusion, f32[32,256,1]{1,0,2:T(8,128)S(1)} %copy-done.6, f32[12,256,256]{2,1,0:T(8,128)S(1)} %get-tuple-element.11, f32[256,256]{1,0:T(8,128)S(1)} %fusion.32, f32[12]{0:T(128)S(1)} %broadcast_multiply_fusion.2), kind=kOutput, calls=%fused_computation.19 | convolution fusion | flops 303661056 | bytes 4227120 | tf_op jit(solution)/shard_map/adjoint_spectra/knxy,cy->knxc/dot_general | solution.py:123
  68.2 3.5 %fusion.12 = f32[12,256,32]{1,2,0:T(8,128)S(1)} fusion(f32[12,256,32]{1,2,0:T(8,128)S(1)} %fusion.1, f32[32,256,1]{1,0,2:T(8,128)S(1)} %copy-done.5, f32[12,256,256]{2,1,0:T(8,128)S(1)} %get-tuple-element.11, f32[256,256]{1,0:T(8,128)S(1)} %fusion.32, f32[12]{0:T(128)S(1)} %broadcast_multiply_fusion.2), kind=kOutput, calls=%fused_computation.18 | convolution fusion | flops 303661056 | bytes 4227120 | tf_op jit(solution)/shard_map/adjoint_spectra/knxy,cy->knxc/dot_general | solution.py:120
  74.9 91.9 %all-reduce.2.cloned.1.call-done = f32[12,2,32,32]{3,2,1,0:T(8,128)} async-done(((f32[12,2,32,32]{3,2,1,0:T(8,128)}), f32[12,2,32,32]{3,2,1,0:T(8,128)}) %all-reduce.2.cloned.1.call-update) | async-done | bytes 98320 | tf_op jit(solution)/shard_map/gradient_exchange/psum | solution.py:148
  166.8 0.9 fusion.61
  167.8 0.9 fusion.24
  169.2 1.0 fusion.53
  170.2 1.0 fusion.22
  171.8 0.9 fusion.62
  172.8 0.9 fusion.23
  173.7 1.1 fusion.16
  174.9 1.0 fusion.54
  175.9 1.0 fusion.21
  176.9 1.4 convolution_add_fusion
  (59 shorter events, 11.4 us)
Async XLA Ops:
  7.2 4.2 %copy-start = (bf16[2,256,256]{2,1,0:T(8,128)(2,1)S(1)}, bf16[2,256,256]{2,1,0:T(8,128)(2,1)}, u32[]{:S(2)}) copy-start(bf16[2,256,256]{2,1,0:T(8,128)(2,1)} %param.10) | copy-start | bytes 786436
  7.2 33.0 %copy-start.6 = (f32[32,256,1]{1,0,2:T(8,128)S(1)}, f32[32,256,1]{1,0,2:T(8,128)}, u32[]{:S(2)}) copy-start(f32[32,256,1]{1,0,2:T(8,128)} %constant.68) | copy-start | bytes 98308
  7.2 33.9 %copy-start.5 = (f32[32,256,1]{1,0,2:T(8,128)S(1)}, f32[32,256,1]{1,0,2:T(8,128)}, u32[]{:S(2)}) copy-start(f32[32,256,1]{1,0,2:T(8,128)} %constant.69) | copy-start | bytes 98308
  7.2 159.6 %all-reduce.2.cloned.1.call-start = ((), (), s32[]{:S(2)}) async-start(), calls=%async_computation | async-start | bytes 786432 | tf_op jit(solution)/shard_map/gradient_exchange/psum | solution.py:148
  40.0 4.8 %copy-start.1 = (f32[1,12,1,32,32]{3,4,1,2,0:T(8,128)}, f32[1,12,1,32,32]{3,4,1,2,0:T(8,128)S(1)}, u32[]{:S(2)}) copy-start(f32[1,12,1,32,32]{3,4,1,2,0:T(8,128)S(1)} %copy.22) | copy-start | bytes 147460
  40.1 4.6 %copy-start.3 = (f32[1,12,1,32,32]{3,4,1,2,0:T(8,128)}, f32[1,12,1,32,32]{3,4,1,2,0:T(8,128)S(1)}, u32[]{:S(2)}) copy-start(f32[1,12,1,32,32]{3,4,1,2,0:T(8,128)S(1)} %copy.23) | copy-start | bytes 147460
  42.0 2.8 %copy-start.7 = (f32[12,256,32]{1,2,0:T(8,128)}, f32[12,256,32]{1,2,0:T(8,128)S(1)}, u32[]{:S(2)}) copy-start(f32[12,256,32]{1,2,0:T(8,128)S(1)} %fusion.15) | copy-start | bytes 1179652
  49.1 3.4 %copy-start.11 = (f32[1,12]{1,0:T(1,128)S(1)}, f32[1,12]{1,0:T(1,128)}, u32[]{:S(2)}) copy-start(f32[1,12]{1,0:T(1,128)} %param.16) | copy-start | bytes 148
  52.5 5.6 %copy-start.10 = (bf16[2,256,256]{2,1,0:T(8,128)(2,1)S(1)}, bf16[2,256,256]{2,1,0:T(8,128)(2,1)}, u32[]{:S(2)}) copy-start(bf16[2,256,256]{2,1,0:T(8,128)(2,1)} %param.12) | copy-start | bytes 786436
  68.1 4.9 %copy-start.2 = (f32[1,12,1,32,32]{3,4,1,2,0:T(8,128)S(1)}, f32[1,12,1,32,32]{3,4,1,2,0:T(8,128)}, u32[]{:S(2)}) copy-start(f32[1,12,1,32,32]{3,4,1,2,0:T(8,128)} %copy-done.1) | copy-start | bytes 147460
  68.1 4.9 %copy-start.4 = (f32[1,12,1,32,32]{3,4,1,2,0:T(8,128)S(1)}, f32[1,12,1,32,32]{3,4,1,2,0:T(8,128)}, u32[]{:S(2)}) copy-start(f32[1,12,1,32,32]{3,4,1,2,0:T(8,128)} %copy-done.3) | copy-start | bytes 147460
  71.6 95.2 %copy-start.9 = (f32[32,256]{1,0:T(8,128)S(1)}, f32[32,256]{1,0:T(8,128)}, u32[]{:S(2)}) copy-start(f32[32,256]{1,0:T(8,128)} %constant.58.clone) | copy-start | bytes 98308
  71.7 96.1 %copy-start.8 = (f32[32,256]{1,0:T(8,128)S(1)}, f32[32,256]{1,0:T(8,128)}, u32[]{:S(2)}) copy-start(f32[32,256]{1,0:T(8,128)} %constant.59.clone) | copy-start | bytes 98308
Sparse Core Ops, SparseCore 0:
  75.0 91.7 all-reduce.1
where the time goes:
time: 187 us; the launch traced here: 185 us
  waiting for transfers between devices  91.9 us (49%)
  matrix products  55.3 us (30%)
  between operations  15.2 us (8%)
  blocking collectives  15.1 us (8%)
  local copies, waits for them, and re-layouts  4.24 us (2%)
  other arithmetic  3.34 us (2%)
    psum x1, waiting for transfers between devices, on_device(): summed = lax.psum(slots, ('tile', 'corner', 'kern'))  91.9 us
    all_gather x1, blocking collectives, on_device(): every = lax.all_gather(own, 'tile', axis=0, tiled=True)  15.1 us
    dot_general x1, matrix products, on_device(): jnp.einsum('knxc,cy->knxy', half_re, sin_tab, precision=precise)  5.58 us
    dot_general x1, matrix products, on_device(): jnp.einsum('knxc,cy->knxy', half_im, cos_tab, precision=precise)  4.34 us
  transfers between devices with their start and end apart: 1, of which 1 were waited for; matrix products, arithmetic and copies ran while one was open for 0% of the time, Pallas kernels for 0%

commit v1 on v0

--- a/solution.py
+++ b/solution.py
@@ -145,7 +145,7 @@
         tile_part = jnp.sum(tile_pick[:, :, None, None, None] * own_grad[:, None], axis=0)
         master_part = jnp.sum(pick[:, :, None, None, None] * own_back[:, None], axis=0)
         slots = jnp.concatenate([tile_part, master_part], axis=0)
-        summed = lax.psum(slots, ("tile", "corner", "kern"))
+        summed = lax.psum(lax.psum(slots, ("corner", "kern")), "tile")
         mine_tiles = lax.dynamic_slice_in_dim(summed, tile_pos * local_tiles, local_tiles, 0)
         mine_masters = lax.dynamic_slice_in_dim(
             summed, region_tiles + tile_pos * local_masters, local_masters, 0

time: 187 us -> 168 us (0.90)
  waiting for transfers between devices: 91.9 us -> 73.6 us
    psum x1 -> x2, waiting for transfers between devices: 91.9 us -> 73.6 us  [on_device(): summed = lax.psum(lax.psum(slots, ('corner', 'kern')), 'tile')]
  transfers between devices with their start and end apart: 1 -> 2, of which waited for: 1 -> 2; matrix products, arithmetic and copies ran while one was open for 0% -> 0% of each run, Pallas kernels for 0% -> 0%
where the time goes in v1:
time: 168 us; the launch traced here: 167 us
  waiting for transfers between devices  73.6 us (44%)
  matrix products  55.3 us (33%)
  between operations  15.2 us (9%)
  blocking collectives  15.1 us (9%)
  local copies, waits for them, and re-layouts  4.24 us (3%)
  other arithmetic  3.34 us (2%)
    psum x2, waiting for transfers between devices, on_device(): summed = lax.psum(lax.psum(slots, ('corner', 'kern')), 'tile')  73.6 us
    all_gather x1, blocking collectives, on_device(): every = lax.all_gather(own, 'tile', axis=0, tiled=True)  15.1 us
    dot_general x1, matrix products, on_device(): jnp.einsum('knxc,cy->knxy', half_re, sin_tab, precision=precise)  5.58 us
    dot_general x1, matrix products, on_device(): jnp.einsum('knxc,cy->knxy', half_im, cos_tab, precision=precise)  4.34 us
    dot_general x1, matrix products, on_device(): jnp.einsum('knxy,cy->knxc', g_im, sin_tab, precision=precise)  3.49 us
  transfers between devices with their start and end apart: 2, of which 2 were waited for; matrix products, arithmetic and copies ran while one was open for 0% of the time, Pallas kernels for 0%

profile of v1, /device:TPU:0, one launch (start us, length us, event | category | flops | bytes accessed | tf_op | source)
XLA Modules:
  0.0 166.9 jit_solution(4923410638888597739)
XLA Ops:
  7.3 1.1 fusion.41
  8.4 1.1 fusion.39
  11.4 1.0 convolution_bitcast_fusion.1
  12.4 1.0 convolution_bitcast_fusion
  16.5 1.3 dynamic_slice.20
  18.5 0.9 fusion.26
  19.4 0.9 fusion.27
  20.4 15.1 %all_gather.3 = f32[4,2,32,32]{3,2,1,0:T(8,128)S(1)} all-gather(f32[1,2,32,32]{3,2,1,0:T(8,128)S(1)} %pad_maximum_fusion.1), channel_id=1, replica_groups=mesh['region'=2,'tile'=4,'corner'=2,'kern'=2] {'tile'}, dimensions={0}, use_global_device_ids=true | all-gather | bytes 40960 | tf_op jit(solution)/shard_map/master_spectra/all_gather | solution.py:76
  35.4 1.3 fusion.75
  36.8 0.9 fusion.28
  37.8 0.9 fusion.25
  38.8 1.1 fusion.77
  42.0 2.7 %fusion.83 = f32[12,256,256]{2,1,0:T(8,128)S(1)} fusion(f32[12,256,32]{1,2,0:T(8,128)S(1)} %fusion.15, f32[32,256,1]{1,0,2:T(8,128)S(1)} %copy-done.6), kind=kOutput, calls=%fused_computation.143 | convolution fusion | flops 301989888 | bytes 3571712 | tf_op jit(solution)/shard_map/forward_fields/knxc,cy->knxy/dot_general | solution.py:106
  44.8 4.3 %fusion.84 = f32[12,256,256]{2,1,0:T(8,128)} fusion(f32[12,256,32]{1,2,0:T(8,128)S(1)} %fusion.14, f32[32,256,1]{1,0,2:T(8,128)S(1)} %copy-done.6), kind=kOutput, calls=%fused_computation.144 | convolution fusion | flops 301989888 | bytes 3571712 | tf_op jit(solution)/shard_map/forward_fields/knxc,cy->knxy/dot_general | solution.py:110
  49.1 2.7 %add_multiply_fusion = f32[12,256,256]{2,1,0:T(8,128)S(1)} fusion(f32[12,256,256]{2,1,0:T(8,128)S(1)} %fusion.83, f32[12,256,32]{1,2,0:T(8,128)S(1)} %fusion.14, f32[32,256,1]{1,0,2:T(8,128)S(1)} %copy-done.5), kind=kOutput, calls=%fused_computation.4 | convolution fusion | flops 303562752 | bytes 6717440 | tf_op jit(solution)/shard_map/forward_fields/knxc,cy->knxy/dot_general | solution.py:107
  52.5 5.6 %multiply_reduce_fusion = (f32[256,256]{1,0:T(8,128)S(1)}, f32[12,256,256]{2,1,0:T(8,128)S(1)}) fusion(f32[12,256,256]{2,1,0:T(8,128)S(1)} %add_multiply_fusion, f32[12]{0:T(128)S(1)} %bitcast.235, f32[12,256,256]{2,1,0:T(8,128)} %fusion.84, f32[12,256,32]{1,2,0:T(8,128)} %copy-done.7, f32[32,256,1]{1,0,2:T(8,128)S(1)} %copy-done.5), kind=kOutput, calls=%fused_computation.2 | convolution fusion | flops 307429376 | bytes 10125360 | tf_op jit(solution)/shard_map/forward_fields/knxc,cy->knxy/dot_general | solution.py:111
  58.3 3.3 %fusion = f32[12,256,32]{1,2,0:T(8,128)S(1)} fusion(f32[32,256,1]{1,0,2:T(8,128)S(1)} %copy-done.5, f32[12,256,256]{2,1,0:T(8,128)S(1)} %add_multiply_fusion, f32[256,256]{1,0:T(8,128)S(1)} %fusion.32, f32[12]{0:T(128)S(1)} %broadcast_multiply_fusion.2), kind=kOutput, calls=%fused_computation.5 | convolution fusion | flops 303562752 | bytes 3833904 | tf_op jit(solution)/shard_map/adjoint_spectra/knxy,cy->knxc/dot_general | solution.py:123
  61.6 3.3 %fusion.1 = f32[12,256,32]{1,2,0:T(8,128)S(1)} fusion(f32[32,256,1]{1,0,2:T(8,128)S(1)} %copy-done.6, f32[12,256,256]{2,1,0:T(8,128)S(1)} %add_multiply_fusion, f32[256,256]{1,0:T(8,128)S(1)} %fusion.32, f32[12]{0:T(128)S(1)} %broadcast_multiply_fusion.2), kind=kOutput, calls=%fused_computation.6 | convolution fusion | flops 303562752 | bytes 3833904 | tf_op jit(solution)/shard_map/adjoint_spectra/knxy,cy->knxc/dot_general | solution.py:120
  64.8 3.3 %fusion.13 = f32[12,256,32]{1,2,0:T(8,128)S(1)} fusion(f32[12,256,32]{1,2,0:T(8,128)S(1)} %fusion, f32[32,256,1]{1,0,2:T(8,128)S(1)} %copy-done.6, f32[12,256,256]{2,1,0:T(8,128)S(1)} %get-tuple-element.11, f32[256,256]{1,0:T(8,128)S(1)} %fusion.32, f32[12]{0:T(128)S(1)} %broadcast_multiply_fusion.2), kind=kOutput, calls=%fused_computation.19 | convolution fusion | flops 303661056 | bytes 4227120 | tf_op jit(solution)/shard_map/adjoint_spectra/knxy,cy->knxc/dot_general | solution.py:123
  68.2 3.5 %fusion.12 = f32[12,256,32]{1,2,0:T(8,128)S(1)} fusion(f32[12,256,32]{1,2,0:T(8,128)S(1)} %fusion.1, f32[32,256,1]{1,0,2:T(8,128)S(1)} %copy-done.5, f32[12,256,256]{2,1,0:T(8,128)S(1)} %get-tuple-element.11, f32[256,256]{1,0:T(8,128)S(1)} %fusion.32, f32[12]{0:T(128)S(1)} %broadcast_multiply_fusion.2), kind=kOutput, calls=%fused_computation.18 | convolution fusion | flops 303661056 | bytes 4227120 | tf_op jit(solution)/shard_map/adjoint_spectra/knxy,cy->knxc/dot_general | solution.py:120
  74.9 34.0 %all-reduce.3.cloned.1.call-done = f32[12,2,32,32]{3,2,1,0:T(8,128)} async-done(((f32[12,2,32,32]{3,2,1,0:T(8,128)}), f32[12,2,32,32]{3,2,1,0:T(8,128)}) %all-reduce.3.cloned.1.call-update) | async-done | bytes 98320 | tf_op jit(solution)/shard_map/gradient_exchange/psum | solution.py:148
  109.0 39.5 %all-reduce.5.cloned.1.call-done = f32[12,2,32,32]{3,2,1,0:T(8,128)} async-done(((f32[12,2,32,32]{3,2,1,0:T(8,128)}), f32[12,2,32,32]{3,2,1,0:T(8,128)}) %all-reduce.5.cloned.1.call-update) | async-done | bytes 98320 | tf_op jit(solution)/shard_map/gradient_exchange/psum | solution.py:148
  148.6 0.9 fusion.61
  149.5 0.9 fusion.24
  150.9 1.0 fusion.53
  151.9 1.0 fusion.22
  153.6 0.9 fusion.62
  154.5 0.9 fusion.23
  155.5 1.1 fusion.16
  156.6 1.0 fusion.54
  157.6 1.0 fusion.21
  158.6 1.4 convolution_add_fusion
  (62 shorter events, 12.4 us)
Async XLA Ops:
  7.2 4.2 %copy-start = (bf16[2,256,256]{2,1,0:T(8,128)(2,1)S(1)}, bf16[2,256,256]{2,1,0:T(8,128)(2,1)}, u32[]{:S(2)}) copy-start(bf16[2,256,256]{2,1,0:T(8,128)(2,1)} %param.10) | copy-start | bytes 786436
  7.2 33.0 %copy-start.6 = (f32[32,256,1]{1,0,2:T(8,128)S(1)}, f32[32,256,1]{1,0,2:T(8,128)}, u32[]{:S(2)}) copy-start(f32[32,256,1]{1,0,2:T(8,128)} %constant.68) | copy-start | bytes 98308
  7.2 33.9 %copy-start.5 = (f32[32,256,1]{1,0,2:T(8,128)S(1)}, f32[32,256,1]{1,0,2:T(8,128)}, u32[]{:S(2)}) copy-start(f32[32,256,1]{1,0,2:T(8,128)} %constant.69) | copy-start | bytes 98308
  7.2 101.8 %all-reduce.3.cloned.1.call-start = ((), (), s32[]{:S(2)}) async-start(), calls=%async_computation | async-start | bytes 786432 | tf_op jit(solution)/shard_map/gradient_exchange/psum | solution.py:148
  40.0 4.8 %copy-start.1 = (f32[1,12,1,32,32]{3,4,1,2,0:T(8,128)}, f32[1,12,1,32,32]{3,4,1,2,0:T(8,128)S(1)}, u32[]{:S(2)}) copy-start(f32[1,12,1,32,32]{3,4,1,2,0:T(8,128)S(1)} %copy.22) | copy-start | bytes 147460
  40.1 4.6 %copy-start.3 = (f32[1,12,1,32,32]{3,4,1,2,0:T(8,128)}, f32[1,12,1,32,32]{3,4,1,2,0:T(8,128)S(1)}, u32[]{:S(2)}) copy-start(f32[1,12,1,32,32]{3,4,1,2,0:T(8,128)S(1)} %copy.23) | copy-start | bytes 147460
  42.0 2.8 %copy-start.7 = (f32[12,256,32]{1,2,0:T(8,128)}, f32[12,256,32]{1,2,0:T(8,128)S(1)}, u32[]{:S(2)}) copy-start(f32[12,256,32]{1,2,0:T(8,128)S(1)} %fusion.15) | copy-start | bytes 1179652
  49.1 3.4 %copy-start.11 = (f32[1,12]{1,0:T(1,128)S(1)}, f32[1,12]{1,0:T(1,128)}, u32[]{:S(2)}) copy-start(f32[1,12]{1,0:T(1,128)} %param.16) | copy-start | bytes 148
  52.5 5.6 %copy-start.10 = (bf16[2,256,256]{2,1,0:T(8,128)(2,1)S(1)}, bf16[2,256,256]{2,1,0:T(8,128)(2,1)}, u32[]{:S(2)}) copy-start(bf16[2,256,256]{2,1,0:T(8,128)(2,1)} %param.12) | copy-start | bytes 786436
  68.1 4.9 %copy-start.2 = (f32[1,12,1,32,32]{3,4,1,2,0:T(8,128)S(1)}, f32[1,12,1,32,32]{3,4,1,2,0:T(8,128)}, u32[]{:S(2)}) copy-start(f32[1,12,1,32,32]{3,4,1,2,0:T(8,128)} %copy-done.1) | copy-start | bytes 147460
  68.1 4.9 %copy-start.4 = (f32[1,12,1,32,32]{3,4,1,2,0:T(8,128)S(1)}, f32[1,12,1,32,32]{3,4,1,2,0:T(8,128)}, u32[]{:S(2)}) copy-start(f32[1,12,1,32,32]{3,4,1,2,0:T(8,128)} %copy-done.3) | copy-start | bytes 147460
  71.6 76.9 %copy-start.9 = (f32[32,256]{1,0:T(8,128)S(1)}, f32[32,256]{1,0:T(8,128)}, u32[]{:S(2)}) copy-start(f32[32,256]{1,0:T(8,128)} %constant.58.clone) | copy-start | bytes 98308
  71.7 77.8 %copy-start.8 = (f32[32,256]{1,0:T(8,128)S(1)}, f32[32,256]{1,0:T(8,128)}, u32[]{:S(2)}) copy-start(f32[32,256]{1,0:T(8,128)} %constant.59.clone) | copy-start | bytes 98308
  74.9 73.7 %all-reduce.5.cloned.1.call-start = ((), (), s32[]{:S(2)}) async-start(), calls=%async_computation.1 | async-start | bytes 786432 | tf_op jit(solution)/shard_map/gradient_exchange/psum | solution.py:148
Sparse Core Ops, SparseCore 0:
  75.0 33.9 all-reduce.2
  111.4 37.0 all-reduce.4
